TPU v7x, 32 devices: a whole 2x2x4 slice. The times are simulated.
32 devices in a mesh: dp: 8 (over y, x, core), tensor: 4 (over z).
Axes of the slice: x: 2, y: 2, z: 4, core: 2. Of those that a mesh axis runs over, the one named last changes fastest.
Arguments:
- inputs: bfloat16 [4096, 2048], P('dp'), may hold values from -6 to 6
- active: int32 [4096], P('dp'), may hold values from 0 to 1, as said below
- block_table: int32 [16], replicated, may hold values from 0 to 15, as said below
- gain_one: bfloat16 [2048], replicated, may hold values from 0.099609375 to 1.8984375
- w_query: bfloat16 [2048, 2048], P(None, 'tensor'), may hold values from -0.125 to 0.125
- w_key: bfloat16 [2048, 1024], P(None, 'tensor'), may hold values from -0.125 to 0.125
- w_value: bfloat16 [2048, 1024], P(None, 'tensor'), may hold values from -0.125 to 0.125
- w_out: bfloat16 [2048, 2048], P('tensor'), may hold values from -4 to 4
- gain_two: bfloat16 [2048], replicated, may hold values from 0.099609375 to 1.8984375
- w_gate: bfloat16 [2048, 5632], P(None, 'tensor'), may hold values from -0.125 to 0.125
- w_up: bfloat16 [2048, 5632], P(None, 'tensor'), may hold values from -0.125 to 0.125
- w_down: bfloat16 [5632, 2048], P('tensor'), may hold values from -0.078125 to 0.078125
- cotangent: bfloat16 [4096, 2048], P('dp'), may hold values from -6 to 6
Outputs:
- output: bfloat16 [4096, 2048], P('dp')
- grad_input: float32 [4096, 2048], P('dp')
- grad_gain_one: float32 [2048], replicated
- grad_w_query: float32 [2048, 2048], P(None, 'tensor')
- grad_w_key: float32 [2048, 1024], P(None, 'tensor')
- grad_w_value: float32 [2048, 1024], P(None, 'tensor')
- grad_w_out: float32 [2048, 2048], P('tensor')
- grad_gain_two: float32 [2048], replicated
- grad_w_gate: float32 [2048, 5632], P(None, 'tensor')
- grad_w_up: float32 [2048, 5632], P(None, 'tensor')
- grad_w_down: float32 [5632, 2048], P('tensor')
Inputs may be any that keep to these rules, and one draw needn't show every extreme that they name: `active`: 0 or 1 for every token; the share of 1s differs from one causal block to another. `block_table`: each causal block appears once; entries 2i and 2i+1 sum to 15.
All inputs are finite; a program needn't handle non-finite values.
Results may differ from a plain program's by a relative error of at most 0.014.
Values may be sent and summed in bfloat16 or wider, within the bound.
No kernel may reach another device: no remote copies, remote signals or barrier semaphores. Data moves between devices by JAX's collectives and lax.ppermute only.
A program may use at most 256 MiB of HBM per device.

v0:
```python
import jax
import jax.numpy as jnp
from jax import lax
from jax.sharding import PartitionSpec as P

HEAD_DIM = 128
EPS = 1e-05
MASKED_SCORE = -1e30


def rms_norm(values, scales):
    return values * lax.rsqrt(jnp.mean(values * values, axis=-1, keepdims=True) + EPS) * scales


def rotate(values, cos_table, sin_table):
    middle = values.shape[-1] // 2
    leading = values[..., :middle]
    trailing = values[..., middle:]
    return jnp.concatenate(
        [leading * cos_table - trailing * sin_table, trailing * cos_table + leading * sin_table],
        axis=-1,
    )


def angles_of(positions, head_size):
    frequency = 10000.0 ** (-jnp.arange(0, head_size, 2, dtype=jnp.float32) / head_size)
    angles = positions.astype(jnp.float32)[:, None] * frequency[None, :]
    return (jnp.cos(angles)[:, None, :], jnp.sin(angles)[:, None, :])


def swiglu(gate_value, up_value):
    return jax.nn.silu(gate_value) * up_value


def left_trans(left, right):
    return lax.dot_general(
        left, right, (((0,), (0,)), ((), ())), preferred_element_type=jnp.float32
    )


def right_trans(left, right):
    return lax.dot_general(
        left, right, (((1,), (1,)), ((), ())), preferred_element_type=jnp.float32
    )


def partner_perm(axis_size, mask):
    return [(index, index ^ mask) for index in range(axis_size)]


def permute_sum(parts, dims, axis):
    size = lax.axis_size(axis)
    steps = size.bit_length() - 1
    assert 1 << steps == size
    me = lax.axis_index(axis)
    pieces = list(parts)
    for step in range(steps):
        bit = me >> step & 1
        keep, send = ([], [])
        for piece, dim in zip(pieces, dims):
            half = piece.shape[dim] // 2
            keep.append(lax.dynamic_slice_in_dim(piece, bit * half, half, axis=dim))
            send.append(
                lax.dynamic_slice_in_dim(piece, (1 - bit) * half, half, axis=dim).astype(
                    jnp.bfloat16
                )
            )
        got = lax.ppermute(send, axis, partner_perm(size, 1 << step))
        pieces = [mine + theirs.astype(jnp.float32) for mine, theirs in zip(keep, got)]
    pieces = [piece.astype(jnp.bfloat16) for piece in pieces]
    for step in reversed(range(steps)):
        first = me >> step & 1 == 0
        got = lax.ppermute(pieces, axis, partner_perm(size, 1 << step))
        pieces = [
            jnp.concatenate(
                [jnp.where(first, mine, theirs), jnp.where(first, theirs, mine)], axis=dim
            )
            for mine, theirs, dim in zip(pieces, got, dims)
        ]
    return [piece.astype(jnp.float32) for piece in pieces]


def permute_allsum(value, axis):
    size = lax.axis_size(axis)
    steps = size.bit_length() - 1
    for step in range(steps):
        value = value + lax.ppermute(value, axis, partner_perm(size, 1 << step))
    return value


def on_device(
    inputs,
    active,
    block_table,
    gain_one,
    w_query,
    w_key,
    w_value,
    w_out,
    gain_two,
    w_gate,
    w_up,
    w_down,
    cotangent,
):
    row_count = inputs.shape[0]
    local_heads = w_query.shape[1] // HEAD_DIM
    local_groups = w_key.shape[1] // HEAD_DIM
    group_size = local_heads // local_groups
    half_rows = row_count // 2
    length = row_count * lax.axis_size("dp")
    score_scale = HEAD_DIM ** (-0.5)
    key_pos = (
        block_table[:, None] * half_rows + jnp.arange(half_rows, dtype=jnp.int32)[None, :]
    ).reshape(length)
    row_start = lax.axis_index("dp") * row_count
    query_pos = lax.dynamic_slice_in_dim(key_pos, row_start, row_count)
    slot_ids = jnp.arange(length, dtype=jnp.int32)
    own_ids = row_start + jnp.arange(row_count, dtype=jnp.int32)
    cos_table, sin_table = angles_of(query_pos, HEAD_DIM)
    keep_rows = active.astype(jnp.float32)[:, None]
    source = inputs.astype(jnp.float32)
    normed_full, norm_one_back = jax.vjp(rms_norm, source, gain_one.astype(jnp.float32))
    normed = normed_full.astype(jnp.bfloat16)
    query_raw = jnp.dot(normed, w_query, preferred_element_type=jnp.float32).reshape(
        row_count, local_heads, HEAD_DIM
    )
    key_raw = jnp.dot(normed, w_key, preferred_element_type=jnp.float32).reshape(
        row_count, local_groups, HEAD_DIM
    )
    value_low = jnp.dot(normed, w_value, preferred_element_type=jnp.float32).astype(jnp.bfloat16)
    query_low = (
        rotate(query_raw, cos_table, sin_table)
        .reshape(row_count, local_heads * HEAD_DIM)
        .astype(jnp.bfloat16)
    )
    key_low = (
        rotate(key_raw, cos_table, sin_table)
        .reshape(row_count, local_groups * HEAD_DIM)
        .astype(jnp.bfloat16)
    )
    alive_low = active.astype(jnp.bfloat16)

    def allowed_of(alive_all):
        return (key_pos[None, :] <= query_pos[:, None]) & (
            (alive_all[None, :] > 0) | (slot_ids[None, :] == own_ids[:, None])
        )

    def head_scores(head_index, keys_all, allowed):
        query_part = query_low[:, head_index * HEAD_DIM : (head_index + 1) * HEAD_DIM]
        group_index = head_index // group_size
        key_part = keys_all[:, group_index * HEAD_DIM : (group_index + 1) * HEAD_DIM]
        raw_scores = right_trans(query_part, key_part) * score_scale
        return jnp.where(allowed, raw_scores, MASKED_SCORE)

    kv_width = local_groups * HEAD_DIM
    all_kv = lax.all_gather(jnp.concatenate([key_low, value_low], axis=1), "dp", axis=0, tiled=True)
    all_keys = all_kv[:, :kv_width]
    all_values = all_kv[:, kv_width:]
    all_alive = lax.all_gather(alive_low, "dp", axis=0, tiled=True)
    allowed_fwd = allowed_of(all_alive)
    mixed_parts = []
    lse_parts = []
    for head_index in range(local_heads):
        masked = head_scores(head_index, all_keys, allowed_fwd)
        row_max = jnp.max(masked, axis=1, keepdims=True)
        shifted = jnp.exp(masked - row_max)
        row_total = jnp.sum(shifted, axis=1, keepdims=True)
        probs_low = (shifted / row_total).astype(jnp.bfloat16)
        lse_parts.append(row_max + jnp.log(row_total))
        group_index = head_index // group_size
        value_part = all_values[:, group_index * HEAD_DIM : (group_index + 1) * HEAD_DIM]
        mixed_parts.append(jnp.dot(probs_low, value_part, preferred_element_type=jnp.float32))
    attended = jnp.concatenate(mixed_parts, axis=1).astype(jnp.bfloat16)
    (branch,) = permute_sum(
        [jnp.dot(attended, w_out, preferred_element_type=jnp.float32)], [0], "tensor"
    )
    middle = source + keep_rows * branch
    normed_two_full, norm_two_back = jax.vjp(rms_norm, middle, gain_two.astype(jnp.float32))
    normed_two = normed_two_full.astype(jnp.bfloat16)
    gate_value = jnp.dot(normed_two, w_gate, preferred_element_type=jnp.float32)
    up_value = jnp.dot(normed_two, w_up, preferred_element_type=jnp.float32)
    hidden_full, swiglu_back = jax.vjp(swiglu, gate_value, up_value)
    hidden = hidden_full.astype(jnp.bfloat16)
    (down_sum,) = permute_sum(
        [jnp.dot(hidden, w_down, preferred_element_type=jnp.float32)], [0], "tensor"
    )
    output = (middle + keep_rows * down_sum).astype(jnp.bfloat16)
    grad_out = cotangent.astype(jnp.float32)
    d_down = (keep_rows * grad_out).astype(jnp.bfloat16)
    grad_w_down = left_trans(hidden, d_down)
    d_hidden = right_trans(d_down, w_down)
    d_gate_full, d_up_full = swiglu_back(d_hidden)
    d_gate = d_gate_full.astype(jnp.bfloat16)
    d_up = d_up_full.astype(jnp.bfloat16)
    grad_w_gate = left_trans(normed_two, d_gate)
    grad_w_up = left_trans(normed_two, d_up)
    (d_normed_two,) = permute_sum(
        [right_trans(d_gate, w_gate) + right_trans(d_up, w_up)], [0], "tensor"
    )
    d_middle_norm, grad_gain_two = norm_two_back(d_normed_two)
    grad_middle = grad_out + d_middle_norm
    d_branch = (keep_rows * grad_middle).astype(jnp.bfloat16)
    grad_w_out = left_trans(attended, d_branch)
    d_attended = right_trans(d_branch, w_out).astype(jnp.bfloat16)
    back_keys, back_values = (all_keys, all_values)
    allowed_back = allowed_fwd
    d_query_parts = []
    d_key_parts = [
        jnp.zeros((length, HEAD_DIM), jnp.float32) for group_index in range(local_groups)
    ]
    d_value_parts = [
        jnp.zeros((length, HEAD_DIM), jnp.float32) for group_index in range(local_groups)
    ]
    for head_index in range(local_heads):
        group_index = head_index // group_size
        masked = head_scores(head_index, back_keys, allowed_back)
        probs = jnp.where(allowed_back, jnp.exp(masked - lse_parts[head_index]), 0.0)
        probs_low = probs.astype(jnp.bfloat16)
        d_out_part = d_attended[:, head_index * HEAD_DIM : (head_index + 1) * HEAD_DIM]
        key_part = back_keys[:, group_index * HEAD_DIM : (group_index + 1) * HEAD_DIM]
        value_part = back_values[:, group_index * HEAD_DIM : (group_index + 1) * HEAD_DIM]
        query_part = query_low[:, head_index * HEAD_DIM : (head_index + 1) * HEAD_DIM]
        d_probs = right_trans(d_out_part, value_part)
        row_delta = jnp.sum(probs * d_probs, axis=1, keepdims=True)
        d_scores = (probs * (d_probs - row_delta)).astype(jnp.bfloat16)
        d_query_parts.append(
            jnp.dot(d_scores, key_part, preferred_element_type=jnp.float32) * score_scale
        )
        d_key_parts[group_index] = (
            d_key_parts[group_index] + left_trans(d_scores, query_part) * score_scale
        )
        d_value_parts[group_index] = d_value_parts[group_index] + left_trans(probs_low, d_out_part)
    d_key_all = jnp.concatenate(d_key_parts, axis=1)
    d_value_all = jnp.concatenate(d_value_parts, axis=1)
    d_kv_own = lax.psum_scatter(
        jnp.concatenate([d_key_all, d_value_all], axis=1).astype(jnp.bfloat16),
        "dp",
        scatter_dimension=0,
        tiled=True,
    ).astype(jnp.float32)
    d_key_own = d_kv_own[:, :kv_width]
    d_value_own = d_kv_own[:, kv_width:]
    d_queries = jnp.concatenate(d_query_parts, axis=1).reshape(row_count, local_heads, HEAD_DIM)
    d_query_low = (
        rotate(d_queries, cos_table, -sin_table)
        .reshape(row_count, local_heads * HEAD_DIM)
        .astype(jnp.bfloat16)
    )
    d_key_low = (
        rotate(d_key_own.reshape(row_count, local_groups, HEAD_DIM), cos_table, -sin_table)
        .reshape(row_count, local_groups * HEAD_DIM)
        .astype(jnp.bfloat16)
    )
    d_value_low = d_value_own.astype(jnp.bfloat16)
    grad_w_query = left_trans(normed, d_query_low)
    grad_w_key = left_trans(normed, d_key_low)
    grad_w_value = left_trans(normed, d_value_low)
    d_normed_part = (
        right_trans(d_query_low, w_query)
        + right_trans(d_key_low, w_key)
        + right_trans(d_value_low, w_value)
    )
    (d_normed,) = permute_sum([d_normed_part], [0], "tensor")
    d_source_norm, grad_gain_one = norm_one_back(d_normed)
    grad_input = grad_middle + d_source_norm
    grad_gain_one = permute_allsum(grad_gain_one, "dp")
    grad_gain_two = permute_allsum(grad_gain_two, "dp")

    def dp_sum(grads):
        return [lax.psum(grad.astype(jnp.bfloat16), "dp").astype(jnp.float32) for grad in grads]

    grad_w_gate, grad_w_up, grad_w_down = dp_sum([grad_w_gate, grad_w_up, grad_w_down])
    grad_w_gate, grad_w_up, grad_w_down, grad_w_out = lax.optimization_barrier(
        (grad_w_gate, grad_w_up, grad_w_down, grad_w_out)
    )
    (grad_w_out,) = dp_sum([grad_w_out])
    grad_w_out, grad_w_query, grad_w_key, grad_w_value = lax.optimization_barrier(
        (grad_w_out, grad_w_query, grad_w_key, grad_w_value)
    )
    grad_w_query, grad_w_key, grad_w_value = dp_sum([grad_w_query, grad_w_key, grad_w_value])
    return (
        output,
        grad_input,
        grad_gain_one,
        grad_w_query,
        grad_w_key,
        grad_w_value,
        grad_w_out,
        grad_gain_two,
        grad_w_gate,
        grad_w_up,
        grad_w_down,
    )


def solution(mesh):
    placed = (
        P("dp", None),
        P("dp"),
        P(),
        P(),
        P(None, "tensor"),
        P(None, "tensor"),
        P(None, "tensor"),
        P("tensor", None),
        P(),
        P(None, "tensor"),
        P(None, "tensor"),
        P("tensor", None),
        P("dp", None),
    )
    return jax.shard_map(
        on_device,
        mesh=mesh,
        in_specs=placed,
        out_specs=(
            P("dp", None),
            P("dp", None),
            P(),
            P(None, "tensor"),
            P(None, "tensor"),
            P(None, "tensor"),
            P("tensor", None),
            P(),
            P(None, "tensor"),
            P(None, "tensor"),
            P("tensor", None),
        ),
        check_vma=False,
    )
```

profile of v0, /device:TPU:0, one launch (start us, length us, event | category | flops | bytes accessed | tf_op | source)
XLA Modules:
  0.0 967.2 jit_solution(9074915309664158548)
XLA Ops:
  10.4 2.8 convolution_convert_fusion.4
  18.5 10.9 %all-gather = bf16[8,1,512]{2,1,0:T(2,128)(2,1)S(1)} all-gather(bf16[1,1,512]{2,1,0:T(2,128)(2,1)S(1)} %reshape.237), channel_id=1, replica_groups=mesh['dp'=8,'tensor'=4] {'dp'}, dimensions={0}, use_global_device_ids=true | all-gather | bytes 9216 | tf_op jit(solution)/shard_map/all_gather | solution.py:160
  29.5 3.7 fusion.102
  33.4 25.2 %all-gather.3.cloned.1.call-done = bf16[4096,512]{0,1:T(8,128)(2,1)} async-done(((bf16[512,512]{0,1:T(8,128)(2,1)}), bf16[4096,512]{0,1:T(8,128)(2,1)}) %all-gather.3.cloned.1.call-update) | async-done | bytes 4194320 | tf_op jit(solution)/shard_map/all_gather | solution.py:157
  58.6 4.7 fusion.110
  63.4 3.4 copy-done.9
  69.0 3.5 fusion.111
  73.8 3.7 fusion.112
  78.8 5.5 fusion.113
  85.6 7.1 fusion.38
  103.9 23.9 %collective-permute-done = bf16[256,2048]{1,0:T(8,128)(2,1)} collective-permute-done((bf16[256,2048]{1,0:T(8,128)(2,1)S(1)}, bf16[256,2048]{1,0:T(8,128)(2,1)}, u32[]{:S(2)}, u32[]{:S(2)}) %collective-permute-start) | collective-permute-done | bytes 1048608 | tf_op jit(solution)/shard_map/ppermute | solution.py:68
  133.9 22.9 %collective-permute-done.1 = bf16[128,2048]{1,0:T(8,128)(2,1)S(1)} collective-permute-done((bf16[128,2048]{1,0:T(8,128)(2,1)S(1)}, bf16[128,2048]{1,0:T(8,128)(2,1)S(1)}, u32[]{:S(2)}, u32[]{:S(2)}) %collective-permute-start.1) | collective-permute-done | bytes 524320 | tf_op jit(solution)/shard_map/ppermute | solution.py:68
  159.0 24.4 %collective-permute-done.2 = bf16[128,2048]{1,0:T(8,128)(2,1)} collective-permute-done((bf16[128,2048]{1,0:T(8,128)(2,1)S(1)}, bf16[128,2048]{1,0:T(8,128)(2,1)}, u32[]{:S(2)}, u32[]{:S(2)}) %collective-permute-start.2) | collective-permute-done | bytes 524320 | tf_op jit(solution)/shard_map/ppermute | solution.py:73
  185.7 6.5 fusion.43
  192.3 17.3 %collective-permute-done.3 = bf16[256,2048]{1,0:T(8,128)(2,1)} collective-permute-done((bf16[256,2048]{1,0:T(8,128)(2,1)}, bf16[256,2048]{1,0:T(8,128)(2,1)}, u32[]{:S(2)}, u32[]{:S(2)}) %collective-permute-start.3) | collective-permute-done | bytes 1048608 | tf_op jit(solution)/shard_map/ppermute | solution.py:73
  213.5 3.4 fusion.114
  216.9 6.0 multiply_convert_fusion.6
  223.0 3.4 fusion.116
  226.5 3.4 convolution_add_fusion.4
  230.4 5.4 fusion.115
  237.8 18.3 %collective-permute-done.8 = bf16[256,2048]{1,0:T(8,128)(2,1)S(1)} collective-permute-done((bf16[256,2048]{1,0:T(8,128)(2,1)S(1)}, bf16[256,2048]{1,0:T(8,128)(2,1)S(1)}, u32[]{:S(2)}, u32[]{:S(2)}) %collective-permute-start.8) | collective-permute-done | bytes 1048608 | tf_op jit(solution)/shard_map/ppermute | solution.py:68
  258.2 28.2 %collective-permute-done.4 = bf16[256,2048]{1,0:T(8,128)(2,1)S(1)} collective-permute-done((bf16[256,2048]{1,0:T(8,128)(2,1)S(1)}, bf16[256,2048]{1,0:T(8,128)(2,1)S(1)}, u32[]{:S(2)}, u32[]{:S(2)}) %collective-permute-start.4) | collective-permute-done | bytes 1048608 | tf_op jit(solution)/shard_map/ppermute | solution.py:68
  286.9 2.5 collective-permute-start.5
  290.1 34.2 %collective-permute-done.5 = bf16[128,2048]{1,0:T(8,128)(2,1)S(1)} collective-permute-done((bf16[128,2048]{1,0:T(8,128)(2,1)S(1)}, bf16[128,2048]{1,0:T(8,128)(2,1)S(1)}, u32[]{:S(2)}, u32[]{:S(2)}) %collective-permute-start.5) | collective-permute-done | bytes 524320 | tf_op jit(solution)/shard_map/ppermute | solution.py:68
  324.5 22.3 %collective-permute-done.10 = bf16[128,2048]{1,0:T(8,128)(2,1)S(1)} collective-permute-done((bf16[128,2048]{1,0:T(8,128)(2,1)S(1)}, bf16[128,2048]{1,0:T(8,128)(2,1)S(1)}, u32[]{:S(2)}, u32[]{:S(2)}) %collective-permute-start.10) | collective-permute-done | bytes 524320 | tf_op jit(solution)/shard_map/ppermute | solution.py:73
  347.1 9.8 %collective-permute-done.6 = bf16[128,2048]{1,0:T(8,128)(2,1)S(1)} collective-permute-done((bf16[128,2048]{1,0:T(8,128)(2,1)S(1)}, bf16[128,2048]{1,0:T(8,128)(2,1)S(1)}, u32[]{:S(2)}, u32[]{:S(2)}) %collective-permute-start.6) | collective-permute-done | bytes 524320 | tf_op jit(solution)/shard_map/ppermute | solution.py:73
  357.2 22.2 %collective-permute-done.11 = bf16[256,2048]{1,0:T(8,128)(2,1)S(1)} collective-permute-done((bf16[256,2048]{1,0:T(8,128)(2,1)S(1)}, bf16[256,2048]{1,0:T(8,128)(2,1)S(1)}, u32[]{:S(2)}, u32[]{:S(2)}) %collective-permute-start.11) | collective-permute-done | bytes 1048608 | tf_op jit(solution)/shard_map/ppermute | solution.py:73
  379.8 3.9 fusion.19
  383.7 18.0 %collective-permute-done.7 = bf16[256,2048]{1,0:T(8,128)(2,1)S(1)} collective-permute-done((bf16[256,2048]{1,0:T(8,128)(2,1)S(1)}, bf16[256,2048]{1,0:T(8,128)(2,1)S(1)}, u32[]{:S(2)}, u32[]{:S(2)}) %collective-permute-start.7) | collective-permute-done | bytes 1048608 | tf_op jit(solution)/shard_map/ppermute | solution.py:73
  402.3 6.1 convert_add_fusion.1
  410.6 3.6 fusion.25
  414.3 3.6 fusion.28
  417.9 4.6 fusion.13
  422.5 4.9 fusion.12
  427.4 4.6 fusion.57
  432.0 4.6 fusion.47
  436.7 4.6 fusion.45
  441.3 20.8 %multiply_reduce_fusion.2 = (f32[512]{0:T(512)S(1)}, f32[512]{0:T(512)S(1)}, f32[512]{0:T(512)S(1)}, f32[512]{0:T(512)}, f32[512,4096]{1,0:T(8,128)}) fusion(f32[512,4096]{1,0:T(8,128)S(1)} %bitcast.53, f32[512]{0:T(512)S(1)} %copy-done.69, s32[512]{0:T(512)S(1)} %copy-done.63, pred[4096]{0:T(1024)(128)(4,1)S(1)} %bitcast.97, s32[512]{0:T(512)S(1)} %copy-done.59, ...), kind=kOutput, calls=%fused_computation.7 | convolution fusion | flops 578811904 | bytes 68329472 | tf_op jit(solution)/shard_map/dot_general | solution.py:42
  462.0 18.5 %multiply_convert_fusion.2 = (bf16[512,4096]{1,0:T(8,128)(2,1)}, bf16[512,4096]{1,0:T(8,128)(2,1)}, bf16[512,4096]{1,0:T(8,128)(2,1)}) fusion(f32[512,4096]{1,0:T(8,128)} %get-tuple-element.88, f32[512]{0:T(512)S(1)} %get-tuple-element.31, f32[512,4096]{1,0:T(8,128)S(1)} %bitcast.53, f32[512]{0:T(512)S(1)} %copy-done.69, s32[512]{0:T(512)S(1)} %copy-done.63, ...), kind=kLoop, calls=%fused_computation.6 | loop fusion | flops 39845888 | bytes 62951424 | tf_op jit(solution)/shard_map/convert_element_type | solution.py:226
  480.6 2.9 fusion.79
  483.6 8.7 multiply_convert_fusion
  500.8 6.8 convolution_convert_fusion.2
  507.6 5.3 convolution_convert_fusion.1
  512.9 5.2 convolution_convert_fusion
  518.3 4.2 convolution_multiply_fusion
  522.8 3.0 convolution_multiply_fusion.1
  525.7 3.0 convolution_multiply_fusion.2
  528.7 2.9 convolution_multiply_fusion.3
  531.9 18.0 %reduce-scatter.2.cloned.1.call-done = bf16[512,512]{0,1:T(8,128)(2,1)} async-done(((bf16[4096,512]{0,1:T(8,128)(2,1)}), bf16[512,512]{0,1:T(8,128)(2,1)}) %reduce-scatter.2.cloned.1.call-update) | async-done | bytes 524304 | tf_op jit(solution)/shard_map/reduce_scatter | solution.py:236
  558.0 23.2 %collective-permute-done.12 = bf16[256,2048]{1,0:T(8,128)(2,1)S(1)} collective-permute-done((bf16[256,2048]{1,0:T(8,128)(2,1)S(1)}, bf16[256,2048]{1,0:T(8,128)(2,1)S(1)}, u32[]{:S(2)}, u32[]{:S(2)}) %collective-permute-start.12) | collective-permute-done | bytes 1048608 | tf_op jit(solution)/shard_map/ppermute | solution.py:68
  586.2 2.8 fusion.97
  589.1 2.7 fusion.87
  591.7 185.1 %all-reduce.10.cloned.1.call-done = (bf16[2048,1408]{1,0:T(8,128)(2,1)}, bf16[2048,1408]{1,0:T(8,128)(2,1)}, bf16[1408,2048]{1,0:T(8,128)(2,1)}) async-done(((bf16[2048,1408]{1,0:T(8,128)(2,1)}, bf16[2048,1408]{1,0:T(8,128)(2,1)}, bf16[1408,2048]{1,0:T(8,128)(2,1)}), (bf16[2048,1408]{1,0:T(8,128)(2,1)}, bf16[2048,1408]{1,0:T(8,128)(2,1)}, bf16[1408,2048]{1,0:T(8,128)(2,1)})) %all-reduce.10.cloned.1.call-update) | async-done | bytes 17301520 | tf_op jit(solution)/shard_map/psum | solution.py:271
  776.8 8.6 convert_element_type.279
  785.4 5.2 convert_element_type.281
  790.6 6.2 convert_element_type.283
  798.4 2.5 collective-permute-start.14
  804.8 54.0 %all-reduce.6.cloned.1.call-done = bf16[512,2048]{1,0:T(8,128)(2,1)} async-done(((bf16[512,2048]{1,0:T(8,128)(2,1)}), bf16[512,2048]{1,0:T(8,128)(2,1)}) %all-reduce.6.cloned.1.call-update) | async-done | bytes 2097168 | tf_op jit(solution)/shard_map/psum | solution.py:271
  858.8 4.1 convert_element_type.285
  867.3 3.3 collective-permute-done.20
  870.9 17.1 %collective-permute-done.15 = bf16[256,2048]{1,0:T(8,128)(2,1)S(1)} collective-permute-done((bf16[256,2048]{1,0:T(8,128)(2,1)S(1)}, bf16[256,2048]{1,0:T(8,128)(2,1)S(1)}, u32[]{:S(2)}, u32[]{:S(2)}) %collective-permute-start.15) | collective-permute-done | bytes 1048608 | tf_op jit(solution)/shard_map/ppermute | solution.py:73
  890.7 52.6 %all-reduce.8.cloned.1.call-done = (bf16[2048,512]{1,0:T(8,128)(2,1)}, bf16[2048,256]{1,0:T(8,128)(2,1)}, bf16[2048,256]{1,0:T(8,128)(2,1)}) async-done(((bf16[2048,512]{1,0:T(8,128)(2,1)}, bf16[2048,256]{1,0:T(8,128)(2,1)}, bf16[2048,256]{1,0:T(8,128)(2,1)}), (bf16[2048,512]{1,0:T(8,128)(2,1)}, bf16[2048,256]{1,0:T(8,128)(2,1)}, bf16[2048,256]{1,0:T(8,128)(2,1)})) %all-reduce.8.cloned.1.call-update) | async-done | bytes 4194320 | tf_op jit(solution)/shard_map/psum | solution.py:271
  943.3 4.3 convert_element_type.287
  955.6 4.2 fusion.21
  (338 shorter events, 93.0 us)
Async XLA Ops:
  7.2 91.7 %copy-start = (bf16[512,2048]{1,0:T(8,128)(2,1)S(1)}, bf16[512,2048]{1,0:T(8,128)(2,1)}, u32[]{:S(2)}) copy-start(bf16[512,2048]{1,0:T(8,128)(2,1)} %param.20) | copy-start | bytes 6291460
  7.2 51.4 %all-gather.3.cloned.1.call-start = ((), (), s32[]{:S(2)}) async-start(), calls=%async_computation.1 | async-start | bytes 4718592 | tf_op jit(solution)/shard_map/all_gather | solution.py:157
  8.1 21.3 %copy-start.55 = (f32[2048]{0:T(1024)}, f32[2048]{0:T(1024)S(1)}, u32[]{:S(2)}) copy-start(f32[2048]{0:T(1024)S(1)} %convert_element_type.224) | copy-start | bytes 24580
  10.4 19.1 %copy-start.72 = (f32[512]{0:T(512)}, f32[512]{0:T(512)S(1)}, u32[]{:S(2)}) copy-start(f32[512]{0:T(512)S(1)} %fusion.90) | copy-start | bytes 6148
  15.2 63.6 %copy-start.57 = (s32[512]{0:T(512)}, s32[512]{0:T(512)S(1)}, u32[]{:S(2)}) copy-start(s32[512]{0:T(512)S(1)} %get-tuple-element.42) | copy-start | bytes 6148
  16.4 16.8 %copy-start.28 = (f32[512,64]{0,1:T(8,128)}, f32[512,64]{0,1:T(8,128)S(1)}, u32[]{:S(2)}) copy-start(f32[512,64]{0,1:T(8,128)S(1)} %get-tuple-element.77) | copy-start | bytes 393220
  18.4 531.5 %reduce-scatter.2.cloned.1.call-start = ((), (), s32[]{:S(2)}) async-start(), calls=%async_computation.2 | async-start | bytes 4718592 | tf_op jit(solution)/shard_map/reduce_scatter | solution.py:236
  29.5 49.3 %copy-start.61 = (s32[512]{0:T(512)}, s32[512]{0:T(512)S(1)}, u32[]{:S(2)}) copy-start(s32[512]{0:T(512)S(1)} %iota_add_fusion) | copy-start | bytes 6148
  33.4 45.4 %copy-start.30 = (bf16[512,4,128]{0,2,1:T(8,128)(2,1)}, bf16[512,4,128]{0,2,1:T(8,128)(2,1)S(1)}, u32[]{:S(2)}) copy-start(bf16[512,4,128]{0,2,1:T(8,128)(2,1)S(1)} %pad_maximum_fusion.8) | copy-start | bytes 1572868
  72.5 20.2 %copy-start.6 = (f32[512,4096]{1,0:T(8,128)}, f32[512,4096]{1,0:T(8,128)S(1)}, u32[]{:S(2)}) copy-start(f32[512,4096]{1,0:T(8,128)S(1)} %get-tuple-element.83) | copy-start | bytes 25165828
  77.5 17.2 %copy-start.7 = (f32[512,4096]{1,0:T(8,128)}, f32[512,4096]{1,0:T(8,128)S(1)}, u32[]{:S(2)}) copy-start(f32[512,4096]{1,0:T(8,128)S(1)} %get-tuple-element.85) | copy-start | bytes 25165828
  84.3 12.5 %copy-start.8 = (f32[512,4096]{1,0:T(8,128)}, f32[512,4096]{1,0:T(8,128)S(1)}, u32[]{:S(2)}) copy-start(f32[512,4096]{1,0:T(8,128)S(1)} %get-tuple-element.87) | copy-start | bytes 25165828
  85.6 7.1 copy-start.26
  92.7 6.1 copy-start.47
  102.3 25.5 %collective-permute-start = (bf16[256,2048]{1,0:T(8,128)(2,1)S(1)}, bf16[256,2048]{1,0:T(8,128)(2,1)}, u32[]{:S(2)}, u32[]{:S(2)}) collective-permute-start(bf16[256,2048]{1,0:T(8,128)(2,1)S(1)} %dynamic-slice_convert_fusion.3), channel_id=1, source_target_pairs={{0,1},{1,0},{2,3},{3,2},{4,5},{5,4},{6,7},{7,6},{8,9},{9,8},{10,11... | collective-permute-start | bytes 3145736 | tf_op jit(solution)/shard_map/ppermute | solution.py:68
  131.3 54.4 %copy-start.80 = (bf16[2048]{0:T(1024)(128)(2,1)S(1)}, bf16[2048]{0:T(1024)(128)(2,1)}, u32[]{:S(2)}) copy-start(bf16[2048]{0:T(1024)(128)(2,1)} %param.21) | copy-start | bytes 12292
  131.4 25.4 %collective-permute-start.1 = (bf16[128,2048]{1,0:T(8,128)(2,1)S(1)}, bf16[128,2048]{1,0:T(8,128)(2,1)S(1)}, u32[]{:S(2)}, u32[]{:S(2)}) collective-permute-start(bf16[128,2048]{1,0:T(8,128)(2,1)S(1)} %dynamic-slice_convert_fusion.7), channel_id=1, source_target_pairs={{0,2},{1,3},{2,0},{3,1},{4,6},{5,7},{6,4},{7,5},{8,10},{9,11},{10,... | collective-permute-start | bytes 1572872 | tf_op jit(solution)/shard_map/ppermute | solution.py:68
  158.2 25.2 %collective-permute-start.2 = (bf16[128,2048]{1,0:T(8,128)(2,1)S(1)}, bf16[128,2048]{1,0:T(8,128)(2,1)}, u32[]{:S(2)}, u32[]{:S(2)}) collective-permute-start(bf16[128,2048]{1,0:T(8,128)(2,1)S(1)} %add_convert_fusion.4), channel_id=1, source_target_pairs={{0,2},{1,3},{2,0},{3,1},{4,6},{5,7},{6,4},{7,5},{8,10},{9,11},{10,... | collective-permute-start | bytes 1572872 | tf_op jit(solution)/shard_map/ppermute | solution.py:73
  185.7 23.8 %collective-permute-start.3 = (bf16[256,2048]{1,0:T(8,128)(2,1)}, bf16[256,2048]{1,0:T(8,128)(2,1)}, u32[]{:S(2)}, u32[]{:S(2)}) collective-permute-start(bf16[256,2048]{1,0:T(8,128)(2,1)} %pad_maximum_fusion.3), channel_id=1, source_target_pairs={{0,1},{1,0},{2,3},{3,2},{4,5},{5,4},{6,7},{7,6},{8,9},{9,8},{10,11... | collective-permute-start | bytes 3145736 | tf_op jit(solution)/shard_map/ppermute | solution.py:73
  192.3 19.2 %copy-start.3 = (bf16[512,2048]{1,0:T(8,128)(2,1)S(1)}, bf16[512,2048]{1,0:T(8,128)(2,1)}, u32[]{:S(2)}) copy-start(bf16[512,2048]{1,0:T(8,128)(2,1)} %param.13) | copy-start | bytes 6291460
  230.1 26.1 %collective-permute-start.8 = (bf16[256,2048]{1,0:T(8,128)(2,1)S(1)}, bf16[256,2048]{1,0:T(8,128)(2,1)S(1)}, u32[]{:S(2)}, u32[]{:S(2)}) collective-permute-start(bf16[256,2048]{1,0:T(8,128)(2,1)S(1)} %dynamic-slice_convert_fusion.1), channel_id=1, source_target_pairs={{0,1},{1,0},{2,3},{3,2},{4,5},{5,4},{6,7},{7,6},{8,9},{9,8},{10,11... | collective-permute-start | bytes 3145736 | tf_op jit(solution)/shard_map/ppermute | solution.py:68
  236.0 50.5 %collective-permute-start.4 = (bf16[256,2048]{1,0:T(8,128)(2,1)S(1)}, bf16[256,2048]{1,0:T(8,128)(2,1)S(1)}, u32[]{:S(2)}, u32[]{:S(2)}) collective-permute-start(bf16[256,2048]{1,0:T(8,128)(2,1)S(1)} %dynamic-slice_convert_fusion.2), channel_id=1, source_target_pairs={{0,1},{1,0},{2,3},{3,2},{4,5},{5,4},{6,7},{7,6},{8,9},{9,8},{10,11... | collective-permute-start | bytes 3145736 | tf_op jit(solution)/shard_map/ppermute | solution.py:68
  256.6 32.9 %collective-permute-start.9 = (bf16[128,2048]{1,0:T(8,128)(2,1)S(1)}, bf16[128,2048]{1,0:T(8,128)(2,1)S(1)}, u32[]{:S(2)}, u32[]{:S(2)}) collective-permute-start(bf16[128,2048]{1,0:T(8,128)(2,1)S(1)} %dynamic-slice_convert_fusion.5), channel_id=1, source_target_pairs={{0,2},{1,3},{2,0},{3,1},{4,6},{5,7},{6,4},{7,5},{8,10},{9,11},{10,... | collective-permute-start | bytes 1572872 | tf_op jit(solution)/shard_map/ppermute | solution.py:68
  286.9 37.4 %collective-permute-start.5 = (bf16[128,2048]{1,0:T(8,128)(2,1)S(1)}, bf16[128,2048]{1,0:T(8,128)(2,1)S(1)}, u32[]{:S(2)}, u32[]{:S(2)}) collective-permute-start(bf16[128,2048]{1,0:T(8,128)(2,1)S(1)} %dynamic-slice_convert_fusion.6), channel_id=1, source_target_pairs={{0,2},{1,3},{2,0},{3,1},{4,6},{5,7},{6,4},{7,5},{8,10},{9,11},{10,... | collective-permute-start | bytes 1572872 | tf_op jit(solution)/shard_map/ppermute | solution.py:68
  289.5 57.2 %collective-permute-start.10 = (bf16[128,2048]{1,0:T(8,128)(2,1)S(1)}, bf16[128,2048]{1,0:T(8,128)(2,1)S(1)}, u32[]{:S(2)}, u32[]{:S(2)}) collective-permute-start(bf16[128,2048]{1,0:T(8,128)(2,1)S(1)} %add_convert_fusion.2), channel_id=1, source_target_pairs={{0,2},{1,3},{2,0},{3,1},{4,6},{5,7},{6,4},{7,5},{8,10},{9,11},{10,... | collective-permute-start | bytes 1572872 | tf_op jit(solution)/shard_map/ppermute | solution.py:73
  324.4 32.4 %collective-permute-start.6 = (bf16[128,2048]{1,0:T(8,128)(2,1)S(1)}, bf16[128,2048]{1,0:T(8,128)(2,1)S(1)}, u32[]{:S(2)}, u32[]{:S(2)}) collective-permute-start(bf16[128,2048]{1,0:T(8,128)(2,1)S(1)} %add_convert_fusion.3), channel_id=1, source_target_pairs={{0,2},{1,3},{2,0},{3,1},{4,6},{5,7},{6,4},{7,5},{8,10},{9,11},{10,... | collective-permute-start | bytes 1572872 | tf_op jit(solution)/shard_map/ppermute | solution.py:73
  346.9 32.4 %collective-permute-start.11 = (bf16[256,2048]{1,0:T(8,128)(2,1)S(1)}, bf16[256,2048]{1,0:T(8,128)(2,1)S(1)}, u32[]{:S(2)}, u32[]{:S(2)}) collective-permute-start(bf16[256,2048]{1,0:T(8,128)(2,1)S(1)} %pad_maximum_fusion.5), channel_id=1, source_target_pairs={{0,1},{1,0},{2,3},{3,2},{4,5},{5,4},{6,7},{7,6},{8,9},{9,8},{10,11... | collective-permute-start | bytes 3145736 | tf_op jit(solution)/shard_map/ppermute | solution.py:73
  347.0 63.5 %copy-start.66 = (f32[512]{0:T(512)}, f32[512]{0:T(512)S(1)}, u32[]{:S(2)}) copy-start(f32[512]{0:T(512)S(1)} %get-tuple-element.90) | copy-start | bytes 6148
  347.0 70.8 %copy-start.74 = (f32[512]{0:T(512)}, f32[512]{0:T(512)S(1)}, u32[]{:S(2)}) copy-start(f32[512]{0:T(512)S(1)} %get-tuple-element.89) | copy-start | bytes 6148
  347.1 67.1 %copy-start.70 = (f32[512]{0:T(512)}, f32[512]{0:T(512)S(1)}, u32[]{:S(2)}) copy-start(f32[512]{0:T(512)S(1)} %get-tuple-element.92) | copy-start | bytes 6148
  347.1 75.4 %copy-start.68 = (f32[512]{0:T(512)}, f32[512]{0:T(512)S(1)}, u32[]{:S(2)}) copy-start(f32[512]{0:T(512)S(1)} %get-tuple-element.91) | copy-start | bytes 6148
  357.1 44.7 %collective-permute-start.7 = (bf16[256,2048]{1,0:T(8,128)(2,1)S(1)}, bf16[256,2048]{1,0:T(8,128)(2,1)S(1)}, u32[]{:S(2)}, u32[]{:S(2)}) collective-permute-start(bf16[256,2048]{1,0:T(8,128)(2,1)S(1)} %pad_maximum_fusion.4), channel_id=1, source_target_pairs={{0,1},{1,0},{2,3},{3,2},{4,5},{5,4},{6,7},{7,6},{8,9},{9,8},{10,11... | collective-permute-start | bytes 3145736 | tf_op jit(solution)/shard_map/ppermute | solution.py:73
  379.8 22.4 %copy-start.32 = (bf16[512,2048]{1,0:T(8,128)(2,1)S(1)}, bf16[512,2048]{1,0:T(8,128)(2,1)}, u32[]{:S(2)}) copy-start(bf16[512,2048]{1,0:T(8,128)(2,1)} %param.25) | copy-start | bytes 6291460
  401.7 8.8 slice-start
  402.3 8.3 slice-start.1
  410.6 7.3 slice-start.6
  410.6 12.0 %slice-start.2 = ((s8[8388608]{0:T(1024)(128)(4,1)}), s8[4194304]{0:T(1024)(128)(4,1)S(1)}, s32[]{:S(2)}) async-start(s8[8388608]{0:T(1024)(128)(4,1)} %bitcast.52), calls=%async_computation.8 | async-start | bytes 8388608
  414.2 8.3 slice-start.3
  462.0 18.6 %copy-start.31 = (bf16[512,4,128]{0,2,1:T(8,128)(2,1)S(1)}, bf16[512,4,128]{0,2,1:T(8,128)(2,1)}, u32[]{:S(2)}) copy-start(bf16[512,4,128]{0,2,1:T(8,128)(2,1)} %copy-done.30) | copy-start | bytes 1572868
  483.6 8.7 copy-start.15
  499.2 8.3 copy-start.84
  499.2 277.6 %all-reduce.10.cloned.1.call-start = ((), (), s32[]{:S(2)}) async-start(), calls=%async_computation.5 | async-start | bytes 34603008 | tf_op jit(solution)/shard_map/psum | solution.py:271
  500.8 6.8 copy-start.37
  518.1 340.8 %all-reduce.6.cloned.1.call-start = ((), (), s32[]{:S(2)}) async-start(), calls=%async_computation.3 | async-start | bytes 4194304 | tf_op jit(solution)/shard_map/psum | solution.py:271
  556.3 30.0 %copy-start.4 = (bf16[512,2048]{1,0:T(8,128)(2,1)S(1)}, bf16[512,2048]{1,0:T(8,128)(2,1)}, u32[]{:S(2)}) copy-start(bf16[512,2048]{1,0:T(8,128)(2,1)} %param.13) | copy-start | bytes 6291460
  556.3 29.9 %copy-start.56 = (f32[2048]{0:T(1024)S(1)}, f32[2048]{0:T(1024)}, u32[]{:S(2)}) copy-start(f32[2048]{0:T(1024)} %copy-done.55) | copy-start | bytes 24580
  556.3 29.9 %copy-start.73 = (f32[512]{0:T(512)S(1)}, f32[512]{0:T(512)}, u32[]{:S(2)}) copy-start(f32[512]{0:T(512)} %copy-done.72) | copy-start | bytes 6148
  556.5 24.8 %collective-permute-start.12 = (bf16[256,2048]{1,0:T(8,128)(2,1)S(1)}, bf16[256,2048]{1,0:T(8,128)(2,1)S(1)}, u32[]{:S(2)}, u32[]{:S(2)}) collective-permute-start(bf16[256,2048]{1,0:T(8,128)(2,1)S(1)} %dynamic-slice_convert_fusion), channel_id=1, source_target_pairs={{0,1},{1,0},{2,3},{3,2},{4,5},{5,4},{6,7},{7,6},{8,9},{9,8},{10,11... | collective-permute-start | bytes 3145736 | tf_op jit(solution)/shard_map/ppermute | solution.py:68
  583.7 213.1 %collective-permute-start.13 = (bf16[128,2048]{1,0:T(8,128)(2,1)}, bf16[128,2048]{1,0:T(8,128)(2,1)}, u32[]{:S(2)}, u32[]{:S(2)}) collective-permute-start(bf16[128,2048]{1,0:T(8,128)(2,1)} %dynamic-slice_convert_fusion.4), channel_id=1, source_target_pairs={{0,2},{1,3},{2,0},{3,1},{4,6},{5,7},{6,4},{7,5},{8,10},{9,11},{10,... | collective-permute-start | bytes 1572872 | tf_op jit(solution)/shard_map/ppermute | solution.py:68
  776.8 8.6 copy-start.24
  776.8 13.8 %slice-start.8 = ((s8[5767168]{0:T(1024)(128)(4,1)}), s8[4194304]{0:T(1024)(128)(4,1)S(1)}, s32[]{:S(2)}) async-start(s8[5767168]{0:T(1024)(128)(4,1)} %bitcast.58), calls=%async_computation.14 | async-start | bytes 8388608
  796.8 146.4 %all-reduce.8.cloned.1.call-start = ((), (), s32[]{:S(2)}) async-start(), calls=%async_computation.4 | async-start | bytes 8388608 | tf_op jit(solution)/shard_map/psum | solution.py:271
  798.4 64.6 %collective-permute-start.14 = (bf16[128,2048]{1,0:T(8,128)(2,1)S(1)}, bf16[128,2048]{1,0:T(8,128)(2,1)}, u32[]{:S(2)}, u32[]{:S(2)}) collective-permute-start(bf16[128,2048]{1,0:T(8,128)(2,1)S(1)} %add_convert_fusion.1), channel_id=1, source_target_pairs={{0,2},{1,3},{2,0},{3,1},{4,6},{5,7},{6,4},{7,5},{8,10},{9,11},{10,... | collective-permute-start | bytes 1572872 | tf_op jit(solution)/shard_map/ppermute | solution.py:73
  864.2 23.8 %collective-permute-start.15 = (bf16[256,2048]{1,0:T(8,128)(2,1)S(1)}, bf16[256,2048]{1,0:T(8,128)(2,1)S(1)}, u32[]{:S(2)}, u32[]{:S(2)}) collective-permute-start(bf16[256,2048]{1,0:T(8,128)(2,1)S(1)} %pad_maximum_fusion.7), channel_id=1, source_target_pairs={{0,1},{1,0},{2,3},{3,2},{4,5},{5,4},{6,7},{7,6},{8,9},{9,8},{10,11... | collective-permute-start | bytes 3145736 | tf_op jit(solution)/shard_map/ppermute | solution.py:73
  865.7 1.2 collective-permute-start.19
  866.9 3.7 collective-permute-start.20
  870.5 19.6 %collective-permute-start.21 = (f32[2048]{0:T(1024)S(1)}, f32[2048]{0:T(1024)S(1)}, u32[]{:S(2)}, u32[]{:S(2)}) collective-permute-start(f32[2048]{0:T(1024)S(1)} %add.262), channel_id=1, source_target_pairs={{0,16},{4,20},{8,24},{12,28},{16,0},{20,4},{24,8},{28,12},{1,17},{... | collective-permute-start | bytes 24584 | tf_op jit(solution)/shard_map/ppermute | solution.py:87
  890.0 60.6 %collective-permute-start.16 = (f32[2048]{0:T(1024)S(1)}, f32[2048]{0:T(1024)S(1)}, u32[]{:S(2)}, u32[]{:S(2)}) collective-permute-start(f32[2048]{0:T(1024)S(1)} %get-tuple-element.29), channel_id=1, source_target_pairs={{0,4},{4,0},{8,12},{12,8},{16,20},{20,16},{24,28},{28,24},{1,5},{5... | collective-permute-start | bytes 24584 | tf_op jit(solution)/shard_map/ppermute | solution.py:87
  943.3 12.3 %copy-start.21 = (bf16[256,2048]{1,0:T(8,128)(2,1)S(1)}, bf16[256,2048]{1,0:T(8,128)(2,1)}, u32[]{:S(2)}) copy-start(bf16[256,2048]{1,0:T(8,128)(2,1)} %copy-done.20) | copy-start | bytes 3145732
  947.6 8.0 copy-start.5
  947.6 8.0 copy-start.12
  950.6 3.7 collective-permute-start.17
  954.3 6.2 copy-start.1
  954.3 5.6 collective-permute-start.18
  (65 other events, 234.6 us)
Sparse Core Ops, SparseCore 0:
  18.5 40.0 all-gather.2
  499.3 50.5 reduce-scatter.1
  554.7 222.0 all-reduce.9
  797.0 61.8 all-reduce.5
  863.1 80.0 all-reduce.7
where the time goes:
time: 971 us; the launch traced here: 967 us
  waiting for transfers between devices  624 us (64%)
  matrix products  170 us (18%)
  other arithmetic  105 us (11%)
  starting transfers between devices  23.2 us (2%)
  local copies, waits for them, and re-layouts  18.1 us (2%)
  between operations  15.7 us (2%)
  blocking collectives  10.9 us (1%)
    psum x3, waiting for transfers between devices, dp_sum(): lax.psum(grad.astype(jnp.bfloat16), 'dp').astype(jnp.float32)  292 us
    ppermute x8, waiting for transfers between devices, permute_sum(): got = lax.ppermute(send, axis, partner_perm(size, 1 << step))  151 us
    ppermute x8, waiting for transfers between devices, permute_sum(): got = lax.ppermute(pieces, axis, partner_perm(size, 1 << step))  131 us
    dot_general x15, matrix products, right_trans(): lax.dot_general(left, right, (((1,), (1,)), ((), ())), preferred_element_...  71 us
    dot_general x15, matrix products, left_trans(): lax.dot_general(left, right, (((0,), (0,)), ((), ())), preferred_element_...  48.8 us
    convert_element_type x7, other arithmetic, dp_sum(): lax.psum(grad.astype(jnp.bfloat16), 'dp').astype(jnp.float32)  31.4 us
    convert_element_type x2, other arithmetic, on_device(): d_scores = (probs * (d_probs - row_delta)).astype(jnp.bfloat16)  27.2 us
    all_gather x1, waiting for transfers between devices, on_device(): lax.all_gather(jnp.concatenate([key_low, value_low], axis=1), 'dp', axis=...  25.2 us
  transfers between devices with their start and end apart: 27, of which 21 were waited for; matrix products, arithmetic and copies ran while one was open for 11% of the time, Pallas kernels for 0%

commit v1 on v0

--- a/solution.py
+++ b/solution.py
@@ -1,3 +1,4 @@
+import functools
 import jax
 import jax.numpy as jnp
 from jax import lax
@@ -6,6 +7,30 @@
 HEAD_DIM = 128
 EPS = 1e-05
 MASKED_SCORE = -1e30
+
+
+def _store_views(frame, axis_no):
+    frame = jnp.moveaxis(frame, 0, axis_no)
+    carry_in = frame.shape
+    return frame.reshape(
+        *carry_in[:axis_no], carry_in[axis_no] * carry_in[axis_no + 1], *carry_in[axis_no + 2 :]
+    )
+
+
+def rest_ends_by_axis(v0, mesh_ax, dim_i):
+    wide_n = jax.lax.axis_size(mesh_ax)
+    steps_seen = [v0]
+    fields = [(u, (u + 1) % wide_n) for u in range(wide_n)]
+    while len(steps_seen) < wide_n:
+        new = jax.lax.ppermute(steps_seen[-1], axis_name=mesh_ax, perm=fields)
+        steps_seen.append(new)
+    b_next = jax.lax.axis_index(mesh_ax)
+    upper = jnp.stack(steps_seen)
+    steps_seen = upper[(b_next - jnp.arange(wide_n)) % wide_n]
+    return _store_views(steps_seen, dim_i)
+
+
+open_the_side = functools.partial(rest_ends_by_axis, mesh_ax="dp", dim_i=0)
 
 
 def rms_norm(values, scales):
@@ -154,7 +179,7 @@
         return jnp.where(allowed, raw_scores, MASKED_SCORE)
 
     kv_width = local_groups * HEAD_DIM
-    all_kv = lax.all_gather(jnp.concatenate([key_low, value_low], axis=1), "dp", axis=0, tiled=True)
+    all_kv = open_the_side(jnp.concatenate([key_low, value_low], axis=1))
     all_keys = all_kv[:, :kv_width]
     all_values = all_kv[:, kv_width:]
     all_alive = lax.all_gather(alive_low, "dp", axis=0, tiled=True)

time: 971 us -> 1020 us (1.050)
  waiting for transfers between devices: 624 us -> 646 us
  local copies, waits for them, and re-layouts: 18.1 us -> 36.8 us
    ppermute x0 -> x7, waiting for transfers between devices: none -> 43.6 us  [rest_ends_by_axis(): new = jax.lax.ppermute(steps_seen[-1], axis_name=mesh_ax, perm=fields)]
    all_gather x1 -> x0, waiting for transfers between devices: 25.2 us -> none  [on_device(): lax.all_gather(jnp.concatenate([key_low, value_low], axis=1), 'dp', axis=...]
    gather x0 -> x2, local copies, waits for them, and re-layouts: none -> 11.5 us  [rest_ends_by_axis(): steps_seen = upper[(b_next - jnp.arange(wide_n)) % wide_n]]
    unnamed x207 -> x211, local copies, waits for them, and re-layouts: 15.5 us -> 22 us
  transfers between devices with their start and end apart: 27 -> 33, of which waited for: 21 -> 26; matrix products, arithmetic and copies ran while one was open for 11% -> 11% of each run, Pallas kernels for 0% -> 0%
where the time goes in v1:
time: 1020 us; the launch traced here: 1010 us
  waiting for transfers between devices  646 us (63%)
  matrix products  166 us (16%)
  other arithmetic  112 us (11%)
  local copies, waits for them, and re-layouts  36.8 us (4%)
  starting transfers between devices  23.8 us (2%)
  between operations  15.6 us (2%)
  blocking collectives  11.7 us (1%)
    psum x3, waiting for transfers between devices, dp_sum(): lax.psum(grad.astype(jnp.bfloat16), 'dp').astype(jnp.float32)  292 us
    ppermute x8, waiting for transfers between devices, permute_sum(): got = lax.ppermute(send, axis, partner_perm(size, 1 << step))  144 us
    ppermute x8, waiting for transfers between devices, permute_sum(): got = lax.ppermute(pieces, axis, partner_perm(size, 1 << step))  132 us
    dot_general x15, matrix products, right_trans(): lax.dot_general(left, right, (((1,), (1,)), ((), ())), preferred_element_...  66.5 us
    dot_general x15, matrix products, left_trans(): lax.dot_general(left, right, (((0,), (0,)), ((), ())), preferred_element_...  54.1 us
    ppermute x7, waiting for transfers between devices, rest_ends_by_axis(): new = jax.lax.ppermute(steps_seen[-1], axis_name=mesh_ax, perm=fields)  43.6 us
    convert_element_type x7, other arithmetic, dp_sum(): lax.psum(grad.astype(jnp.bfloat16), 'dp').astype(jnp.float32)  31.4 us
    reduce_scatter x1, waiting for transfers between devices, on_device(): lax.psum_scatter(jnp.concatenate([d_key_all, d_value_all], axis=1).astype...  27.8 us
  transfers between devices with their start and end apart: 33, of which 26 were waited for; matrix products, arithmetic and copies ran while one was open for 11% of the time, Pallas kernels for 0%

profile of v1, /device:TPU:0, one launch (start us, length us, event | category | flops | bytes accessed | tf_op | source)
XLA Modules:
  0.0 1012.6 jit_solution(16356995346346231810)
XLA Ops:
  16.4 9.7 collective-permute-done
  26.1 9.5 collective-permute-done.1
  36.4 11.7 %all-gather = bf16[8,1,512]{2,1,0:T(2,128)(2,1)S(1)} all-gather(bf16[1,1,512]{2,1,0:T(2,128)(2,1)S(1)} %reshape.298), channel_id=1, replica_groups=mesh['dp'=8,'tensor'=4] {'dp'}, dimensions={0}, use_global_device_ids=true | all-gather | bytes 9216 | tf_op jit(solution)/shard_map/all_gather | solution.py:185
  48.7 4.6 fusion.104
  53.2 4.6 collective-permute-done.3
  60.2 7.5 collective-permute-done.4
  70.2 7.2 collective-permute-done.5
  82.0 4.9 collective-permute-done.6
  87.8 5.0 gather_fusion
  92.8 6.4 copy.25
  99.2 7.8 fusion.112
  107.0 3.8 fusion.113
  110.9 3.8 fusion.114
  114.8 3.8 fusion.115
  118.6 7.8 fusion.5
  126.4 5.4 fusion.38
  133.2 3.2 fusion.39
  150.1 18.9 %collective-permute-done.7 = bf16[256,2048]{1,0:T(8,128)(2,1)} collective-permute-done((bf16[256,2048]{1,0:T(8,128)(2,1)S(1)}, bf16[256,2048]{1,0:T(8,128)(2,1)}, u32[]{:S(2)}, u32[]{:S(2)}) %collective-permute-start.7) | collective-permute-done | bytes 1048608 | tf_op jit(solution)/shard_map/ppermute | solution.py:93
  175.4 18.2 %collective-permute-done.8 = bf16[128,2048]{1,0:T(8,128)(2,1)S(1)} collective-permute-done((bf16[128,2048]{1,0:T(8,128)(2,1)S(1)}, bf16[128,2048]{1,0:T(8,128)(2,1)S(1)}, u32[]{:S(2)}, u32[]{:S(2)}) %collective-permute-start.8) | collective-permute-done | bytes 524320 | tf_op jit(solution)/shard_map/ppermute | solution.py:93
  195.7 24.5 %collective-permute-done.9 = bf16[128,2048]{1,0:T(8,128)(2,1)} collective-permute-done((bf16[128,2048]{1,0:T(8,128)(2,1)S(1)}, bf16[128,2048]{1,0:T(8,128)(2,1)}, u32[]{:S(2)}, u32[]{:S(2)}) %collective-permute-start.9) | collective-permute-done | bytes 524320 | tf_op jit(solution)/shard_map/ppermute | solution.py:98
  222.6 6.5 fusion.43
  229.1 18.0 %collective-permute-done.10 = bf16[256,2048]{1,0:T(8,128)(2,1)} collective-permute-done((bf16[256,2048]{1,0:T(8,128)(2,1)}, bf16[256,2048]{1,0:T(8,128)(2,1)}, u32[]{:S(2)}, u32[]{:S(2)}) %collective-permute-start.10) | collective-permute-done | bytes 1048608 | tf_op jit(solution)/shard_map/ppermute | solution.py:98
  251.1 3.4 fusion.116
  254.6 6.3 multiply_convert_fusion.6
  261.0 3.4 fusion.118
  264.4 5.0 convolution_add_fusion.4
  270.0 3.4 fusion.117
  275.3 26.0 %collective-permute-done.15 = bf16[256,2048]{1,0:T(8,128)(2,1)S(1)} collective-permute-done((bf16[256,2048]{1,0:T(8,128)(2,1)S(1)}, bf16[256,2048]{1,0:T(8,128)(2,1)S(1)}, u32[]{:S(2)}, u32[]{:S(2)}) %collective-permute-start.15) | collective-permute-done | bytes 1048608 | tf_op jit(solution)/shard_map/ppermute | solution.py:93
  301.8 25.0 %collective-permute-done.11 = bf16[256,2048]{1,0:T(8,128)(2,1)S(1)} collective-permute-done((bf16[256,2048]{1,0:T(8,128)(2,1)S(1)}, bf16[256,2048]{1,0:T(8,128)(2,1)S(1)}, u32[]{:S(2)}, u32[]{:S(2)}) %collective-permute-start.11) | collective-permute-done | bytes 1048608 | tf_op jit(solution)/shard_map/ppermute | solution.py:93
  330.4 32.6 %collective-permute-done.12 = bf16[128,2048]{1,0:T(8,128)(2,1)S(1)} collective-permute-done((bf16[128,2048]{1,0:T(8,128)(2,1)S(1)}, bf16[128,2048]{1,0:T(8,128)(2,1)S(1)}, u32[]{:S(2)}, u32[]{:S(2)}) %collective-permute-start.12) | collective-permute-done | bytes 524320 | tf_op jit(solution)/shard_map/ppermute | solution.py:93
  363.2 22.3 %collective-permute-done.17 = bf16[128,2048]{1,0:T(8,128)(2,1)S(1)} collective-permute-done((bf16[128,2048]{1,0:T(8,128)(2,1)S(1)}, bf16[128,2048]{1,0:T(8,128)(2,1)S(1)}, u32[]{:S(2)}, u32[]{:S(2)}) %collective-permute-start.17) | collective-permute-done | bytes 524320 | tf_op jit(solution)/shard_map/ppermute | solution.py:98
  385.8 10.0 collective-permute-done.13
  396.1 22.2 %collective-permute-done.18 = bf16[256,2048]{1,0:T(8,128)(2,1)S(1)} collective-permute-done((bf16[256,2048]{1,0:T(8,128)(2,1)S(1)}, bf16[256,2048]{1,0:T(8,128)(2,1)S(1)}, u32[]{:S(2)}, u32[]{:S(2)}) %collective-permute-start.18) | collective-permute-done | bytes 1048608 | tf_op jit(solution)/shard_map/ppermute | solution.py:98
  418.8 3.9 fusion.19
  422.7 18.0 %collective-permute-done.14 = bf16[256,2048]{1,0:T(8,128)(2,1)S(1)} collective-permute-done((bf16[256,2048]{1,0:T(8,128)(2,1)S(1)}, bf16[256,2048]{1,0:T(8,128)(2,1)S(1)}, u32[]{:S(2)}, u32[]{:S(2)}) %collective-permute-start.14) | collective-permute-done | bytes 1048608 | tf_op jit(solution)/shard_map/ppermute | solution.py:98
  441.2 6.1 convert_add_fusion.1
  453.6 4.5 fusion.45
  458.1 3.6 fusion.25
  461.7 6.3 fusion.28
  468.0 7.5 fusion.13
  475.6 4.6 fusion.12
  480.2 19.7 %multiply_reduce_fusion.2 = (f32[512]{0:T(512)S(1)}, f32[512]{0:T(512)S(1)}, f32[512]{0:T(512)S(1)}, f32[512]{0:T(512)}, f32[512,4096]{1,0:T(8,128)}) fusion(f32[512,4096]{1,0:T(8,128)} %copy-done.7, f32[512]{0:T(512)} %copy-done.72, s32[512]{0:T(512)S(1)} %copy-done.65, pred[4096]{0:T(1024)(128)(4,1)S(1)} %bitcast.129, s32[512]{0:T(512)S(1)} %copy-done.62, ...), kind=kOutput, calls=%fused_computation.8 | convolution fusion | flops 578811904 | bytes 68329472 | tf_op jit(solution)/shard_map/dot_general | solution.py:67
  499.9 18.1 %multiply_convert_fusion.2 = (bf16[512,4096]{1,0:T(8,128)(2,1)}, bf16[512,4096]{1,0:T(8,128)(2,1)}, bf16[512,4096]{1,0:T(8,128)(2,1)}) fusion(f32[512,4096]{1,0:T(8,128)} %get-tuple-element.88, f32[512]{0:T(512)S(1)} %get-tuple-element.31, f32[512,4096]{1,0:T(8,128)} %copy-done.7, f32[512]{0:T(512)S(1)} %copy-done.73, s32[512]{0:T(512)S(1)} %copy-done.65, ...), kind=kLoop, calls=%fused_computation.7 | loop fusion | flops 39845888 | bytes 62951424 | tf_op jit(solution)/shard_map/convert_element_type | solution.py:251
  518.0 3.0 fusion.79
  521.0 9.2 multiply_convert_fusion
  538.6 6.8 convolution_convert_fusion.2
  545.4 5.3 convolution_convert_fusion.1
  550.7 5.2 convolution_convert_fusion
  556.2 4.4 convolution_multiply_fusion
  560.6 2.9 convolution_multiply_fusion.1
  567.5 27.8 %reduce-scatter.2.cloned.1.call-done = bf16[512,512]{0,1:T(8,128)(2,1)} async-done(((bf16[4096,512]{0,1:T(8,128)(2,1)}), bf16[512,512]{0,1:T(8,128)(2,1)}) %reduce-scatter.2.cloned.1.call-update) | async-done | bytes 524304 | tf_op jit(solution)/shard_map/reduce_scatter | solution.py:261
  603.4 23.3 %collective-permute-done.19 = bf16[256,2048]{1,0:T(8,128)(2,1)S(1)} collective-permute-done((bf16[256,2048]{1,0:T(8,128)(2,1)S(1)}, bf16[256,2048]{1,0:T(8,128)(2,1)S(1)}, u32[]{:S(2)}, u32[]{:S(2)}) %collective-permute-start.19) | collective-permute-done | bytes 1048608 | tf_op jit(solution)/shard_map/ppermute | solution.py:93
  631.6 2.8 fusion.99
  637.1 185.1 %all-reduce.10.cloned.1.call-done = (bf16[2048,1408]{1,0:T(8,128)(2,1)}, bf16[2048,1408]{1,0:T(8,128)(2,1)}, bf16[1408,2048]{1,0:T(8,128)(2,1)}) async-done(((bf16[2048,1408]{1,0:T(8,128)(2,1)}, bf16[2048,1408]{1,0:T(8,128)(2,1)}, bf16[1408,2048]{1,0:T(8,128)(2,1)}), (bf16[2048,1408]{1,0:T(8,128)(2,1)}, bf16[2048,1408]{1,0:T(8,128)(2,1)}, bf16[1408,2048]{1,0:T(8,128)(2,1)})) %all-reduce.10.cloned.1.call-update) | async-done | bytes 17301520 | tf_op jit(solution)/shard_map/psum | solution.py:296
  822.2 8.6 convert_element_type.279
  830.8 5.2 convert_element_type.281
  836.0 6.2 convert_element_type.283
  850.2 54.0 %all-reduce.6.cloned.1.call-done = bf16[512,2048]{1,0:T(8,128)(2,1)} async-done(((bf16[512,2048]{1,0:T(8,128)(2,1)}), bf16[512,2048]{1,0:T(8,128)(2,1)}) %all-reduce.6.cloned.1.call-update) | async-done | bytes 2097168 | tf_op jit(solution)/shard_map/psum | solution.py:296
  904.2 4.1 convert_element_type.285
  912.6 3.3 collective-permute-done.27
  916.3 17.1 %collective-permute-done.22 = bf16[256,2048]{1,0:T(8,128)(2,1)S(1)} collective-permute-done((bf16[256,2048]{1,0:T(8,128)(2,1)S(1)}, bf16[256,2048]{1,0:T(8,128)(2,1)S(1)}, u32[]{:S(2)}, u32[]{:S(2)}) %collective-permute-start.22) | collective-permute-done | bytes 1048608 | tf_op jit(solution)/shard_map/ppermute | solution.py:98
  936.0 52.6 %all-reduce.8.cloned.1.call-done = (bf16[2048,512]{1,0:T(8,128)(2,1)}, bf16[2048,256]{1,0:T(8,128)(2,1)}, bf16[2048,256]{1,0:T(8,128)(2,1)}) async-done(((bf16[2048,512]{1,0:T(8,128)(2,1)}, bf16[2048,256]{1,0:T(8,128)(2,1)}, bf16[2048,256]{1,0:T(8,128)(2,1)}), (bf16[2048,512]{1,0:T(8,128)(2,1)}, bf16[2048,256]{1,0:T(8,128)(2,1)}, bf16[2048,256]{1,0:T(8,128)(2,1)})) %all-reduce.8.cloned.1.call-update) | async-done | bytes 4194320 | tf_op jit(solution)/shard_map/psum | solution.py:296
  988.6 4.3 convert_element_type.287
  1001.0 4.2 fusion.21
  (359 shorter events, 116.5 us)
Async XLA Ops:
  7.2 136.9 %copy-start = (bf16[512,2048]{1,0:T(8,128)(2,1)S(1)}, bf16[512,2048]{1,0:T(8,128)(2,1)}, u32[]{:S(2)}) copy-start(bf16[512,2048]{1,0:T(8,128)(2,1)} %param.20) | copy-start | bytes 6291460
  7.2 588.1 %reduce-scatter.2.cloned.1.call-start = ((), (), s32[]{:S(2)}) async-start(), calls=%async_computation.1 | async-start | bytes 4718592 | tf_op jit(solution)/shard_map/reduce_scatter | solution.py:261
  8.1 40.5 %copy-start.59 = (f32[2048]{0:T(1024)}, f32[2048]{0:T(1024)S(1)}, u32[]{:S(2)}) copy-start(f32[2048]{0:T(1024)S(1)} %convert_element_type.224) | copy-start | bytes 24580
  10.4 38.2 %copy-start.74 = (f32[512]{0:T(512)}, f32[512]{0:T(512)S(1)}, u32[]{:S(2)}) copy-start(f32[512]{0:T(512)S(1)} %fusion.90) | copy-start | bytes 6148
  13.3 23.1 %copy-start.83 = (s32[512]{0:T(512)S(1)}, s32[512]{0:T(512)}, u32[]{:S(2)}) copy-start(s32[512]{0:T(512)} %param.14) | copy-start | bytes 6148
  14.4 100.3 %copy-start.61 = (s32[512]{0:T(512)}, s32[512]{0:T(512)S(1)}, u32[]{:S(2)}) copy-start(s32[512]{0:T(512)S(1)} %get-tuple-element.42) | copy-start | bytes 6148
  14.4 100.3 %copy-start.64 = (s32[512]{0:T(512)}, s32[512]{0:T(512)S(1)}, u32[]{:S(2)}) copy-start(s32[512]{0:T(512)S(1)} %get-tuple-element.89) | copy-start | bytes 6148
  15.7 43.1 %copy-start.28 = (f32[512,64]{0,1:T(8,128)}, f32[512,64]{0,1:T(8,128)S(1)}, u32[]{:S(2)}) copy-start(f32[512,64]{0,1:T(8,128)S(1)} %get-tuple-element.77) | copy-start | bytes 393220
  15.8 10.3 %collective-permute-start = (bf16[512,512]{0,1:T(8,128)(2,1)S(1)}, bf16[512,512]{0,1:T(8,128)(2,1)S(1)}, u32[]{:S(2)}, u32[]{:S(2)}) collective-permute-start(bf16[512,512]{0,1:T(8,128)(2,1)S(1)} %pad_maximum_fusion.9), channel_id=1, source_target_pairs={{0,4},{4,8},{8,12},{12,16},{16,20},{20,24},{24,28},{28,0},{1,5},{5... | collective-permute-start | bytes 1572872 | tf_op jit(solution)/shard_map/ppermute | solution.py:25
  26.1 9.5 collective-permute-start.1
  36.4 11.8 %collective-permute-start.2 = (bf16[512,512]{0,1:T(8,128)(2,1)S(1)}, bf16[512,512]{0,1:T(8,128)(2,1)S(1)}, u32[]{:S(2)}, u32[]{:S(2)}) collective-permute-start(bf16[512,512]{0,1:T(8,128)(2,1)S(1)} %collective-permute-done.1), channel_id=1, source_target_pairs={{0,4},{4,8},{8,12},{12,16},{16,20},{20,24},{24,28},{28,0},{1,5},{5... | collective-permute-start | bytes 1572872 | tf_op jit(solution)/shard_map/ppermute | solution.py:25
  48.2 9.7 collective-permute-start.3
  57.9 9.8 collective-permute-start.4
  57.9 10.6 %copy-start.48 = (bf16[512,512]{0,1:T(8,128)(2,1)S(1)}, bf16[512,512]{0,1:T(8,128)(2,1)}, u32[]{:S(2)}) copy-start(bf16[512,512]{0,1:T(8,128)(2,1)} %copy-done.47) | copy-start | bytes 1572868
  57.9 11.4 %copy-start.50 = (bf16[512,512]{0,1:T(8,128)(2,1)S(1)}, bf16[512,512]{0,1:T(8,128)(2,1)}, u32[]{:S(2)}) copy-start(bf16[512,512]{0,1:T(8,128)(2,1)} %copy-done.49) | copy-start | bytes 1572868
  60.2 54.5 %copy-start.30 = (bf16[512,4,128]{0,2,1:T(8,128)(2,1)}, bf16[512,4,128]{0,2,1:T(8,128)(2,1)S(1)}, u32[]{:S(2)}) copy-start(bf16[512,4,128]{0,2,1:T(8,128)(2,1)S(1)} %pad_maximum_fusion.8) | copy-start | bytes 1572868
  67.7 9.7 collective-permute-start.5
  77.4 9.5 collective-permute-start.6
  110.9 22.3 %copy-start.6 = (f32[512,4096]{1,0:T(8,128)}, f32[512,4096]{1,0:T(8,128)S(1)}, u32[]{:S(2)}) copy-start(f32[512,4096]{1,0:T(8,128)S(1)} %get-tuple-element.83) | copy-start | bytes 25165828
  114.8 23.0 %copy-start.7 = (f32[512,4096]{1,0:T(8,128)}, f32[512,4096]{1,0:T(8,128)S(1)}, u32[]{:S(2)}) copy-start(f32[512,4096]{1,0:T(8,128)S(1)} %get-tuple-element.85) | copy-start | bytes 25165828
  118.6 23.4 %copy-start.8 = (f32[512,4096]{1,0:T(8,128)}, f32[512,4096]{1,0:T(8,128)S(1)}, u32[]{:S(2)}) copy-start(f32[512,4096]{1,0:T(8,128)S(1)} %get-tuple-element.87) | copy-start | bytes 25165828
  131.9 12.2 %copy-start.51 = (bf16[512,128]{0,1:T(8,128)(2,1)}, bf16[512,128]{0,1:T(8,128)(2,1)S(1)}, u32[]{:S(2)}) copy-start(bf16[512,128]{0,1:T(8,128)(2,1)S(1)} %fusion.38) | copy-start | bytes 393220
  147.6 21.4 %collective-permute-start.7 = (bf16[256,2048]{1,0:T(8,128)(2,1)S(1)}, bf16[256,2048]{1,0:T(8,128)(2,1)}, u32[]{:S(2)}, u32[]{:S(2)}) collective-permute-start(bf16[256,2048]{1,0:T(8,128)(2,1)S(1)} %dynamic-slice_convert_fusion.3), channel_id=1, source_target_pairs={{0,1},{1,0},{2,3},{3,2},{4,5},{5,4},{6,7},{7,6},{8,9},{9,8},{10,11... | collective-permute-start | bytes 3145736 | tf_op jit(solution)/shard_map/ppermute | solution.py:93
  172.6 50.0 %copy-start.82 = (bf16[2048]{0:T(1024)(128)(2,1)S(1)}, bf16[2048]{0:T(1024)(128)(2,1)}, u32[]{:S(2)}) copy-start(bf16[2048]{0:T(1024)(128)(2,1)} %param.21) | copy-start | bytes 12292
  172.6 21.0 %collective-permute-start.8 = (bf16[128,2048]{1,0:T(8,128)(2,1)S(1)}, bf16[128,2048]{1,0:T(8,128)(2,1)S(1)}, u32[]{:S(2)}, u32[]{:S(2)}) collective-permute-start(bf16[128,2048]{1,0:T(8,128)(2,1)S(1)} %dynamic-slice_convert_fusion.7), channel_id=1, source_target_pairs={{0,2},{1,3},{2,0},{3,1},{4,6},{5,7},{6,4},{7,5},{8,10},{9,11},{10,... | collective-permute-start | bytes 1572872 | tf_op jit(solution)/shard_map/ppermute | solution.py:93
  194.9 25.3 %collective-permute-start.9 = (bf16[128,2048]{1,0:T(8,128)(2,1)S(1)}, bf16[128,2048]{1,0:T(8,128)(2,1)}, u32[]{:S(2)}, u32[]{:S(2)}) collective-permute-start(bf16[128,2048]{1,0:T(8,128)(2,1)S(1)} %add_convert_fusion.4), channel_id=1, source_target_pairs={{0,2},{1,3},{2,0},{3,1},{4,6},{5,7},{6,4},{7,5},{8,10},{9,11},{10,... | collective-permute-start | bytes 1572872 | tf_op jit(solution)/shard_map/ppermute | solution.py:98
  222.6 24.6 %collective-permute-start.10 = (bf16[256,2048]{1,0:T(8,128)(2,1)}, bf16[256,2048]{1,0:T(8,128)(2,1)}, u32[]{:S(2)}, u32[]{:S(2)}) collective-permute-start(bf16[256,2048]{1,0:T(8,128)(2,1)} %pad_maximum_fusion.3), channel_id=1, source_target_pairs={{0,1},{1,0},{2,3},{3,2},{4,5},{5,4},{6,7},{7,6},{8,9},{9,8},{10,11... | collective-permute-start | bytes 3145736 | tf_op jit(solution)/shard_map/ppermute | solution.py:98
  229.1 20.0 %copy-start.3 = (bf16[512,2048]{1,0:T(8,128)(2,1)S(1)}, bf16[512,2048]{1,0:T(8,128)(2,1)}, u32[]{:S(2)}) copy-start(bf16[512,2048]{1,0:T(8,128)(2,1)} %param.13) | copy-start | bytes 6291460
  269.6 31.7 %collective-permute-start.15 = (bf16[256,2048]{1,0:T(8,128)(2,1)S(1)}, bf16[256,2048]{1,0:T(8,128)(2,1)S(1)}, u32[]{:S(2)}, u32[]{:S(2)}) collective-permute-start(bf16[256,2048]{1,0:T(8,128)(2,1)S(1)} %dynamic-slice_convert_fusion.1), channel_id=1, source_target_pairs={{0,1},{1,0},{2,3},{3,2},{4,5},{5,4},{6,7},{7,6},{8,9},{9,8},{10,11... | collective-permute-start | bytes 3145736 | tf_op jit(solution)/shard_map/ppermute | solution.py:93
  273.5 53.3 %collective-permute-start.11 = (bf16[256,2048]{1,0:T(8,128)(2,1)S(1)}, bf16[256,2048]{1,0:T(8,128)(2,1)S(1)}, u32[]{:S(2)}, u32[]{:S(2)}) collective-permute-start(bf16[256,2048]{1,0:T(8,128)(2,1)S(1)} %dynamic-slice_convert_fusion.2), channel_id=1, source_target_pairs={{0,1},{1,0},{2,3},{3,2},{4,5},{5,4},{6,7},{7,6},{8,9},{9,8},{10,11... | collective-permute-start | bytes 3145736 | tf_op jit(solution)/shard_map/ppermute | solution.py:93
  275.3 182.7 %copy-start.68 = (f32[512]{0:T(512)}, f32[512]{0:T(512)S(1)}, u32[]{:S(2)}) copy-start(f32[512]{0:T(512)S(1)} %log_add_fusion.1) | copy-start | bytes 6148
  301.7 26.4 %collective-permute-start.16 = (bf16[128,2048]{1,0:T(8,128)(2,1)S(1)}, bf16[128,2048]{1,0:T(8,128)(2,1)S(1)}, u32[]{:S(2)}, u32[]{:S(2)}) collective-permute-start(bf16[128,2048]{1,0:T(8,128)(2,1)S(1)} %dynamic-slice_convert_fusion.5), channel_id=1, source_target_pairs={{0,2},{1,3},{2,0},{3,1},{4,6},{5,7},{6,4},{7,5},{8,10},{9,11},{10,... | collective-permute-start | bytes 1572872 | tf_op jit(solution)/shard_map/ppermute | solution.py:93
  327.2 35.8 %collective-permute-start.12 = (bf16[128,2048]{1,0:T(8,128)(2,1)S(1)}, bf16[128,2048]{1,0:T(8,128)(2,1)S(1)}, u32[]{:S(2)}, u32[]{:S(2)}) collective-permute-start(bf16[128,2048]{1,0:T(8,128)(2,1)S(1)} %dynamic-slice_convert_fusion.6), channel_id=1, source_target_pairs={{0,2},{1,3},{2,0},{3,1},{4,6},{5,7},{6,4},{7,5},{8,10},{9,11},{10,... | collective-permute-start | bytes 1572872 | tf_op jit(solution)/shard_map/ppermute | solution.py:93
  328.3 57.2 %collective-permute-start.17 = (bf16[128,2048]{1,0:T(8,128)(2,1)S(1)}, bf16[128,2048]{1,0:T(8,128)(2,1)S(1)}, u32[]{:S(2)}, u32[]{:S(2)}) collective-permute-start(bf16[128,2048]{1,0:T(8,128)(2,1)S(1)} %add_convert_fusion.2), channel_id=1, source_target_pairs={{0,2},{1,3},{2,0},{3,1},{4,6},{5,7},{6,4},{7,5},{8,10},{9,11},{10,... | collective-permute-start | bytes 1572872 | tf_op jit(solution)/shard_map/ppermute | solution.py:98
  330.4 137.6 %copy-start.76 = (f32[512]{0:T(512)}, f32[512]{0:T(512)S(1)}, u32[]{:S(2)}) copy-start(f32[512]{0:T(512)S(1)} %log_add_fusion) | copy-start | bytes 6148
  363.2 32.7 %collective-permute-start.13 = (bf16[128,2048]{1,0:T(8,128)(2,1)S(1)}, bf16[128,2048]{1,0:T(8,128)(2,1)S(1)}, u32[]{:S(2)}, u32[]{:S(2)}) collective-permute-start(bf16[128,2048]{1,0:T(8,128)(2,1)S(1)} %add_convert_fusion.3), channel_id=1, source_target_pairs={{0,2},{1,3},{2,0},{3,1},{4,6},{5,7},{6,4},{7,5},{8,10},{9,11},{10,... | collective-permute-start | bytes 1572872 | tf_op jit(solution)/shard_map/ppermute | solution.py:98
  385.7 32.6 %collective-permute-start.18 = (bf16[256,2048]{1,0:T(8,128)(2,1)S(1)}, bf16[256,2048]{1,0:T(8,128)(2,1)S(1)}, u32[]{:S(2)}, u32[]{:S(2)}) collective-permute-start(bf16[256,2048]{1,0:T(8,128)(2,1)S(1)} %pad_maximum_fusion.5), channel_id=1, source_target_pairs={{0,1},{1,0},{2,3},{3,2},{4,5},{5,4},{6,7},{7,6},{8,9},{9,8},{10,11... | collective-permute-start | bytes 3145736 | tf_op jit(solution)/shard_map/ppermute | solution.py:98
  385.7 75.9 %copy-start.70 = (f32[512]{0:T(512)}, f32[512]{0:T(512)S(1)}, u32[]{:S(2)}) copy-start(f32[512]{0:T(512)S(1)} %log_add_fusion.3) | copy-start | bytes 6148
  385.8 89.8 %copy-start.72 = (f32[512]{0:T(512)}, f32[512]{0:T(512)S(1)}, u32[]{:S(2)}) copy-start(f32[512]{0:T(512)S(1)} %log_add_fusion.2) | copy-start | bytes 6148
  396.0 44.7 %collective-permute-start.14 = (bf16[256,2048]{1,0:T(8,128)(2,1)S(1)}, bf16[256,2048]{1,0:T(8,128)(2,1)S(1)}, u32[]{:S(2)}, u32[]{:S(2)}) collective-permute-start(bf16[256,2048]{1,0:T(8,128)(2,1)S(1)} %pad_maximum_fusion.4), channel_id=1, source_target_pairs={{0,1},{1,0},{2,3},{3,2},{4,5},{5,4},{6,7},{7,6},{8,9},{9,8},{10,11... | collective-permute-start | bytes 3145736 | tf_op jit(solution)/shard_map/ppermute | solution.py:98
  418.8 22.4 %copy-start.32 = (bf16[512,2048]{1,0:T(8,128)(2,1)S(1)}, bf16[512,2048]{1,0:T(8,128)(2,1)}, u32[]{:S(2)}) copy-start(bf16[512,2048]{1,0:T(8,128)(2,1)} %param.25) | copy-start | bytes 6291460
  458.1 17.5 %slice-start.2 = ((s8[8388608]{0:T(1024)(128)(4,1)}), s8[4194304]{0:T(1024)(128)(4,1)S(1)}, s32[]{:S(2)}) async-start(s8[8388608]{0:T(1024)(128)(4,1)} %bitcast.71), calls=%async_computation.7 | async-start | bytes 8388608
  461.7 13.9 %slice-start.3 = ((s8[8388608]{0:T(1024)(128)(4,1)}), s8[4194304]{0:T(1024)(128)(4,1)S(1)}, s32[]{:S(2)}) async-start(s8[8388608]{0:T(1024)(128)(4,1)} %bitcast.71), calls=%async_computation.8 | async-start | bytes 8388608
  480.2 19.7 %copy-start.73 = (f32[512]{0:T(512)S(1)}, f32[512]{0:T(512)}, u32[]{:S(2)}) copy-start(f32[512]{0:T(512)} %copy-done.72) | copy-start | bytes 6148
  499.9 18.1 %copy-start.31 = (bf16[512,4,128]{0,2,1:T(8,128)(2,1)S(1)}, bf16[512,4,128]{0,2,1:T(8,128)(2,1)}, u32[]{:S(2)}) copy-start(bf16[512,4,128]{0,2,1:T(8,128)(2,1)} %copy-done.30) | copy-start | bytes 1572868
  521.0 9.2 copy-start.11
  537.1 285.1 %all-reduce.10.cloned.1.call-start = ((), (), s32[]{:S(2)}) async-start(), calls=%async_computation.4 | async-start | bytes 34603008 | tf_op jit(solution)/shard_map/psum | solution.py:296
  555.9 348.2 %all-reduce.6.cloned.1.call-start = ((), (), s32[]{:S(2)}) async-start(), calls=%async_computation.2 | async-start | bytes 4194304 | tf_op jit(solution)/shard_map/psum | solution.py:296
  601.6 29.9 %copy-start.4 = (bf16[512,2048]{1,0:T(8,128)(2,1)S(1)}, bf16[512,2048]{1,0:T(8,128)(2,1)}, u32[]{:S(2)}) copy-start(bf16[512,2048]{1,0:T(8,128)(2,1)} %param.13) | copy-start | bytes 6291460
  601.6 29.9 %copy-start.60 = (f32[2048]{0:T(1024)S(1)}, f32[2048]{0:T(1024)}, u32[]{:S(2)}) copy-start(f32[2048]{0:T(1024)} %copy-done.59) | copy-start | bytes 24580
  601.7 29.9 %copy-start.75 = (f32[512]{0:T(512)S(1)}, f32[512]{0:T(512)}, u32[]{:S(2)}) copy-start(f32[512]{0:T(512)} %copy-done.74) | copy-start | bytes 6148
  601.8 24.8 %collective-permute-start.19 = (bf16[256,2048]{1,0:T(8,128)(2,1)S(1)}, bf16[256,2048]{1,0:T(8,128)(2,1)S(1)}, u32[]{:S(2)}, u32[]{:S(2)}) collective-permute-start(bf16[256,2048]{1,0:T(8,128)(2,1)S(1)} %dynamic-slice_convert_fusion), channel_id=1, source_target_pairs={{0,1},{1,0},{2,3},{3,2},{4,5},{5,4},{6,7},{7,6},{8,9},{9,8},{10,11... | collective-permute-start | bytes 3145736 | tf_op jit(solution)/shard_map/ppermute | solution.py:93
  629.1 213.1 %collective-permute-start.20 = (bf16[128,2048]{1,0:T(8,128)(2,1)}, bf16[128,2048]{1,0:T(8,128)(2,1)}, u32[]{:S(2)}, u32[]{:S(2)}) collective-permute-start(bf16[128,2048]{1,0:T(8,128)(2,1)} %dynamic-slice_convert_fusion.4), channel_id=1, source_target_pairs={{0,2},{1,3},{2,0},{3,1},{4,6},{5,7},{6,4},{7,5},{8,10},{9,11},{10,... | collective-permute-start | bytes 1572872 | tf_op jit(solution)/shard_map/ppermute | solution.py:93
  822.2 13.8 %slice-start.4 = ((s8[5767168]{0:T(1024)(128)(4,1)}), s8[4194304]{0:T(1024)(128)(4,1)S(1)}, s32[]{:S(2)}) async-start(s8[5767168]{0:T(1024)(128)(4,1)} %bitcast.89), calls=%async_computation.9 | async-start | bytes 8388608
  842.2 146.4 %all-reduce.8.cloned.1.call-start = ((), (), s32[]{:S(2)}) async-start(), calls=%async_computation.3 | async-start | bytes 8388608 | tf_op jit(solution)/shard_map/psum | solution.py:296
  843.8 64.6 %collective-permute-start.21 = (bf16[128,2048]{1,0:T(8,128)(2,1)S(1)}, bf16[128,2048]{1,0:T(8,128)(2,1)}, u32[]{:S(2)}, u32[]{:S(2)}) collective-permute-start(bf16[128,2048]{1,0:T(8,128)(2,1)S(1)} %add_convert_fusion.1), channel_id=1, source_target_pairs={{0,2},{1,3},{2,0},{3,1},{4,6},{5,7},{6,4},{7,5},{8,10},{9,11},{10,... | collective-permute-start | bytes 1572872 | tf_op jit(solution)/shard_map/ppermute | solution.py:98
  909.6 23.8 %collective-permute-start.22 = (bf16[256,2048]{1,0:T(8,128)(2,1)S(1)}, bf16[256,2048]{1,0:T(8,128)(2,1)S(1)}, u32[]{:S(2)}, u32[]{:S(2)}) collective-permute-start(bf16[256,2048]{1,0:T(8,128)(2,1)S(1)} %pad_maximum_fusion.7), channel_id=1, source_target_pairs={{0,1},{1,0},{2,3},{3,2},{4,5},{5,4},{6,7},{7,6},{8,9},{9,8},{10,11... | collective-permute-start | bytes 3145736 | tf_op jit(solution)/shard_map/ppermute | solution.py:98
  911.0 1.2 collective-permute-start.26
  912.2 3.7 collective-permute-start.27
  915.9 19.6 %collective-permute-start.28 = (f32[2048]{0:T(1024)S(1)}, f32[2048]{0:T(1024)S(1)}, u32[]{:S(2)}, u32[]{:S(2)}) collective-permute-start(f32[2048]{0:T(1024)S(1)} %add.287), channel_id=1, source_target_pairs={{0,16},{4,20},{8,24},{12,28},{16,0},{20,4},{24,8},{28,12},{1,17},{... | collective-permute-start | bytes 24584 | tf_op jit(solution)/shard_map/ppermute | solution.py:112
  935.3 60.6 %collective-permute-start.23 = (f32[2048]{0:T(1024)S(1)}, f32[2048]{0:T(1024)S(1)}, u32[]{:S(2)}, u32[]{:S(2)}) collective-permute-start(f32[2048]{0:T(1024)S(1)} %get-tuple-element.29), channel_id=1, source_target_pairs={{0,4},{4,0},{8,12},{12,8},{16,20},{20,16},{24,28},{28,24},{1,5},{5... | collective-permute-start | bytes 24584 | tf_op jit(solution)/shard_map/ppermute | solution.py:112
  988.6 12.3 %copy-start.24 = (bf16[256,2048]{1,0:T(8,128)(2,1)S(1)}, bf16[256,2048]{1,0:T(8,128)(2,1)}, u32[]{:S(2)}) copy-start(bf16[256,2048]{1,0:T(8,128)(2,1)} %copy-done.23) | copy-start | bytes 3145732
  995.9 3.7 collective-permute-start.24
  999.6 5.6 collective-permute-start.25
  (70 other events, 294.8 us)
Sparse Core Ops, SparseCore 0:
  537.2 58.0 reduce-scatter.1
  600.1 222.0 all-reduce.9
  842.3 61.8 all-reduce.5
  908.5 80.0 all-reduce.7
